TPU v7x, 32 devices: a whole 2x2x4 slice. The times are simulated.
32 devices in a mesh: section: 4 (over y, x), expert: 8 (over z, core).
Axes of the slice: x: 2, y: 2, z: 4, core: 2. Of those that a mesh axis runs over, the one named last changes fastest.
Arguments:
- tokens: bfloat16 [4, 128, 2048], P(None, 'expert'), may hold values from -6 to 6
- norm_gain: float32 [4, 2048], P('section'), may hold values from 0.1 to 1.9
- gate_weight: bfloat16 [4, 16, 2048, 768], P('section', 'expert'), may hold values from -0.125 to 0.125
- up_weight: bfloat16 [4, 16, 2048, 768], P('section', 'expert'), may hold values from -0.125 to 0.125
- down_weight: bfloat16 [4, 16, 768, 2048], P('section', 'expert'), may hold values from -0.21875 to 0.21875
- routes: int32 [4, 4, 128, 8], P('section', None, 'expert'), may hold values from 0 to 15, all different within a row; in each aligned block of 16 rows (0 to 15, 16 to 31, ..., all dimensions but the last counted through in order) at most 12 rows name the same one
- gates: float32 [4, 4, 128, 8], P('section', None, 'expert'), may hold values from 0.1 to 1
Outputs:
- hidden_states: bfloat16 [4, 4, 128, 2048], P('section', None, 'expert')
Inputs may be any that keep to these rules, and one draw needn't show every extreme that they name: `routes`: within one section and micro-batch, the 16 tokens of one device name any one expert at most 12 times, a bound that some expert reaches in some of these blocks; the 8 experts of a token differ.
All inputs are finite; a program needn't handle non-finite values.
Results may differ from a plain program's by a relative error of at most 0.012.
Values may be sent and summed in bfloat16 or wider, within the bound.
No kernel may reach another device: no remote copies, remote signals or barrier semaphores. Data moves between devices by JAX's collectives and lax.ppermute only.
A program may use at most 128 MiB of HBM per device.

v0:
```python
import jax
import jax.numpy as jnp
from jax import lax
from jax.sharding import PartitionSpec as P

MB = 4
EPSILON = 1e-06


def shifted(array, axis, by):
    count = lax.axis_size(axis)
    pairs = [(i, i + by) for i in range(count) if 0 <= i + by < count]
    return lax.ppermute(array, axis, pairs)


def rms_normed(hidden, gain):
    values = hidden.astype(jnp.float32)
    scale = lax.rsqrt(jnp.mean(values * values, axis=-1, keepdims=True) + EPSILON)
    return (values, (values * scale * gain).astype(jnp.bfloat16))


def route_weights(routes, gates, first_expert, local_experts):
    weights = gates / jnp.sum(gates, axis=-1, keepdims=True)
    mine = first_expert + jnp.arange(local_experts, dtype=jnp.int32)
    hit = routes[..., None] == mine
    return jnp.sum(jnp.where(hit, weights[..., None], 0.0), axis=-2)


def on_device(tokens, norm_gain, gate_weight, up_weight, down_weight, routes, gates):
    sections = lax.axis_size("section")
    section_index = lax.axis_index("section")
    expert_index = lax.axis_index("expert")
    local_experts = gate_weight.shape[1]
    gain = norm_gain[0]
    w_gate = gate_weight[0]
    w_up = up_weight[0]
    w_down = down_weight[0]
    all_routes = lax.all_gather(routes[0], "expert", axis=1, tiled=True)
    all_gates = lax.all_gather(gates[0], "expert", axis=1, tiled=True)
    mixing = route_weights(all_routes, all_gates, expert_index * local_experts, local_experts)
    tok_rows = tokens.shape[1]
    width = tokens.shape[2]
    held = jnp.zeros((tok_rows, width), jnp.bfloat16)
    collected = jnp.zeros((MB, tok_rows, width), jnp.bfloat16)
    for moment in range(MB + sections - 1):
        if moment > 0:
            arrived = shifted(held, "section", 1)
        else:
            arrived = held
        batch_index = moment - section_index
        active = (batch_index >= 0) & (batch_index < MB)
        clipped = jnp.clip(batch_index, 0, MB - 1)
        first_rows = lax.dynamic_index_in_dim(tokens, clipped, 0, keepdims=False)
        incoming = jnp.where(section_index == 0, first_rows, arrived)
        weight = lax.dynamic_index_in_dim(mixing, clipped, 0, keepdims=False)
        values, normed = rms_normed(incoming, gain)
        rows = lax.all_gather(normed, "expert", axis=0, tiled=True)
        gate_part = jnp.einsum("td,edf->etf", rows, w_gate, preferred_element_type=jnp.float32)
        up_part = jnp.einsum("td,edf->etf", rows, w_up, preferred_element_type=jnp.float32)
        inner = (jax.nn.silu(gate_part) * up_part).astype(jnp.bfloat16)
        expert_out = jnp.einsum(
            "etf,efd->etd", inner, w_down, preferred_element_type=jnp.float32
        ).astype(jnp.bfloat16)
        partial = jnp.sum(weight.T[:, :, None] * expert_out.astype(jnp.float32), axis=0)
        mixed = lax.psum_scatter(partial, "expert", scatter_dimension=0, tiled=True)
        produced = (values + mixed).astype(jnp.bfloat16)
        held = jnp.where(active, produced, incoming)
        updated = lax.dynamic_update_index_in_dim(collected, held, clipped, 0)
        collected = jnp.where(active, updated, collected)
    return collected[None]


def solution(mesh):
    placed = (
        P(None, "expert", None),
        P("section", None),
        P("section", "expert", None, None),
        P("section", "expert", None, None),
        P("section", "expert", None, None),
        P("section", None, "expert", None),
        P("section", None, "expert", None),
    )
    return jax.shard_map(
        on_device,
        mesh=mesh,
        in_specs=placed,
        out_specs=P("section", None, "expert", None),
        check_vma=False,
    )
```

profile of v0, /device:TPU:0, one launch (start us, length us, event | category | flops | bytes accessed | tf_op | source)
XLA Modules:
  0.0 498.8 jit_solution(13108458287692976375)
XLA Ops:
  7.3 15.9 %all-gather.1 = f32[1,4,128,8]{3,1,0,2:T(4,128)S(1)} all-gather(f32[1,4,16,8]{3,1,0,2:T(4,128)S(1)} %copy.16), channel_id=3, replica_groups=mesh['section'=4,'expert'=8] {'expert'}, dimensions={2}, use_global_device_ids=true | all-gather | bytes 18432 | tf_op jit(solution)/shard_map/all_gather | solution.py:39
  24.5 14.2 %all-gather = s32[1,4,128,8]{3,1,0,2:T(4,128)S(1)} all-gather(s32[1,4,16,8]{3,1,0,2:T(4,128)S(1)} %copy.14), channel_id=2, replica_groups=mesh['section'=4,'expert'=8] {'expert'}, dimensions={2}, use_global_device_ids=true | all-gather | bytes 18432 | tf_op jit(solution)/shard_map/all_gather | solution.py:38
  38.8 1.0 fusion.287
  39.8 0.9 fusion.289
  40.8 14.8 %all_gather.29 = bf16[128,2048]{1,0:T(8,128)(2,1)S(1)} all-gather(bf16[16,2048]{1,0:T(8,128)(2,1)S(1)} %fusion.289), channel_id=1, replica_groups=mesh['section'=4,'expert'=8] {'expert'}, dimensions={0}, use_global_device_ids=true | all-gather | bytes 589824 | tf_op jit(solution)/shard_map/all_gather | solution.py:57
  55.6 3.8 fusion.126
  59.5 7.8 %fusion.123 = f32[128,2048]{1,0:T(8,128)} fusion(bf16[1,2,768,2048]{3,2,1,0:T(8,128)(2,1)} %param.11, f32[2,128]{1,0:T(2,128)S(1)} %get-tuple-element.35, bf16[1,2,2048,768]{3,2,1,0:T(8,128)(2,1)} %param.10, f32[2,128,768]{2,1,0:T(8,128)S(1)} %fusion.126, bf16[128,2048]{1,0:T(8,128)(2,1)S(1)} %all_gather.29), kind=kOutput, calls=%fused_computation.69 | convolution fusion | flops 1613627392 | bytes 14943232 | tf_op jit(solution)/shard_map/etf,efd->etd/dot_general | solution.py:61
  67.4 33.9 %reduce-scatter.8.cloned.1.call-done = f32[16,2048]{1,0:T(8,128)} async-done(((f32[128,2048]{1,0:T(8,128)}), f32[16,2048]{1,0:T(8,128)}) %reduce-scatter.8.cloned.1.call-update) | async-done | bytes 131088 | tf_op jit(solution)/shard_map/reduce_scatter | solution.py:65
  101.3 0.9 bitcast_dynamic-update-slice_fusion
  102.2 3.4 collective-permute-start
  105.7 1.9 collective-permute-done
  107.8 15.0 %all_gather.30 = bf16[128,2048]{1,0:T(8,128)(2,1)S(1)} all-gather(bf16[16,2048]{1,0:T(8,128)(2,1)S(1)} %fusion.293), channel_id=1, replica_groups=mesh['section'=4,'expert'=8] {'expert'}, dimensions={0}, use_global_device_ids=true | all-gather | bytes 589824 | tf_op jit(solution)/shard_map/all_gather | solution.py:57
  122.8 3.8 fusion.129
  126.6 7.8 %fusion.120 = f32[128,2048]{1,0:T(8,128)} fusion(bf16[1,2,768,2048]{3,2,1,0:T(8,128)(2,1)} %param.11, f32[2,128]{1,0:T(2,128)S(1)} %get-tuple-element.34, bf16[1,2,2048,768]{3,2,1,0:T(8,128)(2,1)} %param.10, f32[2,128,768]{2,1,0:T(8,128)S(1)} %fusion.129, bf16[128,2048]{1,0:T(8,128)(2,1)S(1)} %all_gather.30), kind=kOutput, calls=%fused_computation.68 | convolution fusion | flops 1613627392 | bytes 14943232 | tf_op jit(solution)/shard_map/etf,efd->etd/dot_general | solution.py:61
  134.4 31.6 %reduce-scatter.10.cloned.1.call-done = f32[16,2048]{1,0:T(8,128)} async-done(((f32[128,2048]{1,0:T(8,128)}), f32[16,2048]{1,0:T(8,128)}) %reduce-scatter.10.cloned.1.call-update) | async-done | bytes 131088 | tf_op jit(solution)/shard_map/reduce_scatter | solution.py:65
  167.0 3.2 collective-permute-start.1
  170.2 1.9 collective-permute-done.1
  172.3 15.2 %all_gather.31 = bf16[128,2048]{1,0:T(8,128)(2,1)S(1)} all-gather(bf16[16,2048]{1,0:T(8,128)(2,1)S(1)} %fusion.297), channel_id=1, replica_groups=mesh['section'=4,'expert'=8] {'expert'}, dimensions={0}, use_global_device_ids=true | all-gather | bytes 589824 | tf_op jit(solution)/shard_map/all_gather | solution.py:57
  187.5 3.8 fusion.132
  191.3 7.8 %fusion.117 = f32[128,2048]{1,0:T(8,128)} fusion(bf16[1,2,768,2048]{3,2,1,0:T(8,128)(2,1)} %param.11, f32[2,128]{1,0:T(2,128)S(1)} %get-tuple-element.33, bf16[1,2,2048,768]{3,2,1,0:T(8,128)(2,1)} %param.10, f32[2,128,768]{2,1,0:T(8,128)S(1)} %fusion.132, bf16[128,2048]{1,0:T(8,128)(2,1)S(1)} %all_gather.31), kind=kOutput, calls=%fused_computation.67 | convolution fusion | flops 1613627392 | bytes 14943232 | tf_op jit(solution)/shard_map/etf,efd->etd/dot_general | solution.py:61
  199.2 31.7 %reduce-scatter.12.cloned.1.call-done = f32[16,2048]{1,0:T(8,128)} async-done(((f32[128,2048]{1,0:T(8,128)}), f32[16,2048]{1,0:T(8,128)}) %reduce-scatter.12.cloned.1.call-update) | async-done | bytes 131088 | tf_op jit(solution)/shard_map/reduce_scatter | solution.py:65
  230.9 0.9 fusion.329
  231.9 3.6 collective-permute-start.2
  235.5 1.9 collective-permute-done.2
  237.6 15.0 %all_gather.32 = bf16[128,2048]{1,0:T(8,128)(2,1)S(1)} all-gather(bf16[16,2048]{1,0:T(8,128)(2,1)S(1)} %fusion.301), channel_id=1, replica_groups=mesh['section'=4,'expert'=8] {'expert'}, dimensions={0}, use_global_device_ids=true | all-gather | bytes 589824 | tf_op jit(solution)/shard_map/all_gather | solution.py:57
  252.6 3.8 fusion.135
  256.4 7.8 %fusion.114 = f32[128,2048]{1,0:T(8,128)} fusion(bf16[1,2,768,2048]{3,2,1,0:T(8,128)(2,1)} %param.11, f32[2,128]{1,0:T(2,128)S(1)} %get-tuple-element.32, bf16[1,2,2048,768]{3,2,1,0:T(8,128)(2,1)} %param.10, f32[2,128,768]{2,1,0:T(8,128)S(1)} %fusion.135, bf16[128,2048]{1,0:T(8,128)(2,1)S(1)} %all_gather.32), kind=kOutput, calls=%fused_computation.66 | convolution fusion | flops 1613627392 | bytes 14943232 | tf_op jit(solution)/shard_map/etf,efd->etd/dot_general | solution.py:61
  264.3 31.5 %reduce-scatter.14.cloned.1.call-done = f32[16,2048]{1,0:T(8,128)} async-done(((f32[128,2048]{1,0:T(8,128)}), f32[16,2048]{1,0:T(8,128)}) %reduce-scatter.14.cloned.1.call-update) | async-done | bytes 131088 | tf_op jit(solution)/shard_map/reduce_scatter | solution.py:65
  295.8 0.9 fusion.328
  296.7 3.7 collective-permute-start.3
  300.4 1.9 collective-permute-done.3
  302.5 15.0 %all_gather.33 = bf16[128,2048]{1,0:T(8,128)(2,1)S(1)} all-gather(bf16[16,2048]{1,0:T(8,128)(2,1)S(1)} %fusion.305), channel_id=1, replica_groups=mesh['section'=4,'expert'=8] {'expert'}, dimensions={0}, use_global_device_ids=true | all-gather | bytes 589824 | tf_op jit(solution)/shard_map/all_gather | solution.py:57
  317.6 3.8 fusion.138
  321.4 7.8 %fusion.111 = f32[128,2048]{1,0:T(8,128)} fusion(bf16[1,2,768,2048]{3,2,1,0:T(8,128)(2,1)} %param.11, f32[2,128]{1,0:T(2,128)S(1)} %get-tuple-element.31, bf16[1,2,2048,768]{3,2,1,0:T(8,128)(2,1)} %param.10, f32[2,128,768]{2,1,0:T(8,128)S(1)} %fusion.138, bf16[128,2048]{1,0:T(8,128)(2,1)S(1)} %all_gather.33), kind=kOutput, calls=%fused_computation.65 | convolution fusion | flops 1613627392 | bytes 14943232 | tf_op jit(solution)/shard_map/etf,efd->etd/dot_general | solution.py:61
  329.2 31.7 %reduce-scatter.16.cloned.1.call-done = f32[16,2048]{1,0:T(8,128)} async-done(((f32[128,2048]{1,0:T(8,128)}), f32[16,2048]{1,0:T(8,128)}) %reduce-scatter.16.cloned.1.call-update) | async-done | bytes 131088 | tf_op jit(solution)/shard_map/reduce_scatter | solution.py:65
  361.8 3.3 collective-permute-start.4
  365.2 1.9 collective-permute-done.4
  367.3 15.2 %all_gather.34 = bf16[128,2048]{1,0:T(8,128)(2,1)S(1)} all-gather(bf16[16,2048]{1,0:T(8,128)(2,1)S(1)} %fusion.309), channel_id=1, replica_groups=mesh['section'=4,'expert'=8] {'expert'}, dimensions={0}, use_global_device_ids=true | all-gather | bytes 589824 | tf_op jit(solution)/shard_map/all_gather | solution.py:57
  382.5 3.8 fusion.141
  386.3 7.8 %fusion.108 = f32[128,2048]{1,0:T(8,128)} fusion(bf16[1,2,768,2048]{3,2,1,0:T(8,128)(2,1)} %param.11, f32[2,128]{1,0:T(2,128)S(1)} %get-tuple-element.30, bf16[1,2,2048,768]{3,2,1,0:T(8,128)(2,1)} %param.10, f32[2,128,768]{2,1,0:T(8,128)S(1)} %fusion.141, bf16[128,2048]{1,0:T(8,128)(2,1)S(1)} %all_gather.34), kind=kOutput, calls=%fused_computation.64 | convolution fusion | flops 1613627392 | bytes 14943232 | tf_op jit(solution)/shard_map/etf,efd->etd/dot_general | solution.py:61
  394.1 31.5 %reduce-scatter.18.cloned.1.call-done = f32[16,2048]{1,0:T(8,128)} async-done(((f32[128,2048]{1,0:T(8,128)}), f32[16,2048]{1,0:T(8,128)}) %reduce-scatter.18.cloned.1.call-update) | async-done | bytes 131088 | tf_op jit(solution)/shard_map/reduce_scatter | solution.py:65
  426.5 3.7 collective-permute-start.5
  430.2 1.9 collective-permute-done.5
  432.3 15.0 %all_gather.35 = bf16[128,2048]{1,0:T(8,128)(2,1)S(1)} all-gather(bf16[16,2048]{1,0:T(8,128)(2,1)S(1)} %fusion.313), channel_id=1, replica_groups=mesh['section'=4,'expert'=8] {'expert'}, dimensions={0}, use_global_device_ids=true | all-gather | bytes 589824 | tf_op jit(solution)/shard_map/all_gather | solution.py:57
  447.4 3.8 fusion.144
  451.1 7.8 %fusion.105 = f32[128,2048]{1,0:T(8,128)} fusion(bf16[1,2,768,2048]{3,2,1,0:T(8,128)(2,1)} %param.11, f32[2,128]{1,0:T(2,128)S(1)} %get-tuple-element.29, bf16[1,2,2048,768]{3,2,1,0:T(8,128)(2,1)} %param.10, f32[2,128,768]{2,1,0:T(8,128)S(1)} %fusion.144, bf16[128,2048]{1,0:T(8,128)(2,1)S(1)} %all_gather.35), kind=kOutput, calls=%fused_computation.63 | convolution fusion | flops 1613627392 | bytes 14943232 | tf_op jit(solution)/shard_map/etf,efd->etd/dot_general | solution.py:61
  459.6 30.7 %reduce-scatter.20.cloned.1.call-done = f32[16,2048]{1,0:T(8,128)} async-done(((f32[128,2048]{1,0:T(8,128)}), f32[16,2048]{1,0:T(8,128)}) %reduce-scatter.20.cloned.1.call-update) | async-done | bytes 131088 | tf_op jit(solution)/shard_map/reduce_scatter | solution.py:65
  490.4 1.6 fusion.325
  (51 shorter events, 7.6 us)
Async XLA Ops:
  6.5 94.7 %reduce-scatter.8.cloned.1.call-start = ((), (), s32[]{:S(2)}) async-start(), calls=%async_computation.7 | async-start | bytes 1179648 | tf_op jit(solution)/shard_map/reduce_scatter | solution.py:65
  59.5 41.8 %copy-start = (bf16[4,16,2048]{2,1,0:T(8,128)(2,1)S(1)}, bf16[4,16,2048]{2,1,0:T(8,128)(2,1)}, u32[]{:S(2)}) copy-start(bf16[4,16,2048]{2,1,0:T(8,128)(2,1)} %param.7) | copy-start | bytes 786436
  59.5 48.2 %copy-start.1 = (f32[1,2048]{1,0:T(1,128)S(1)}, f32[1,2048]{1,0:T(1,128)}, u32[]{:S(2)}) copy-start(f32[1,2048]{1,0:T(1,128)} %param.8) | copy-start | bytes 24580
  67.3 98.7 %reduce-scatter.10.cloned.1.call-start = ((), (), s32[]{:S(2)}) async-start(), calls=%async_computation.8 | async-start | bytes 1179648 | tf_op jit(solution)/shard_map/reduce_scatter | solution.py:65
  102.2 5.3 %collective-permute-start = (bf16[16,2048]{1,0:T(8,128)(2,1)S(1)}, bf16[16,2048]{1,0:T(8,128)(2,1)S(1)}, u32[]{:S(2)}, u32[]{:S(2)}) collective-permute-start(bf16[16,2048]{1,0:T(8,128)(2,1)S(1)} %get-tuple-element.28), channel_id=1, source_target_pairs={{0,8},{8,16},{16,24},{1,9},{9,17},{17,25},{2,10},{10,18},{18,26},{... | collective-permute-start | bytes 196616 | tf_op jit(solution)/shard_map/ppermute | solution.py:13
  134.4 96.5 %reduce-scatter.12.cloned.1.call-start = ((), (), s32[]{:S(2)}) async-start(), calls=%async_computation.9 | async-start | bytes 1179648 | tf_op jit(solution)/shard_map/reduce_scatter | solution.py:65
  167.0 5.1 %collective-permute-start.1 = (bf16[16,2048]{1,0:T(8,128)(2,1)S(1)}, bf16[16,2048]{1,0:T(8,128)(2,1)S(1)}, u32[]{:S(2)}, u32[]{:S(2)}) collective-permute-start(bf16[16,2048]{1,0:T(8,128)(2,1)S(1)} %get-tuple-element.24), channel_id=1, source_target_pairs={{0,8},{8,16},{16,24},{1,9},{9,17},{17,25},{2,10},{10,18},{18,26},{... | collective-permute-start | bytes 196616 | tf_op jit(solution)/shard_map/ppermute | solution.py:13
  199.1 96.7 %reduce-scatter.14.cloned.1.call-start = ((), (), s32[]{:S(2)}) async-start(), calls=%async_computation.10 | async-start | bytes 1179648 | tf_op jit(solution)/shard_map/reduce_scatter | solution.py:65
  231.9 5.5 %collective-permute-start.2 = (bf16[16,2048]{1,0:T(8,128)(2,1)S(1)}, bf16[16,2048]{1,0:T(8,128)(2,1)S(1)}, u32[]{:S(2)}, u32[]{:S(2)}) collective-permute-start(bf16[16,2048]{1,0:T(8,128)(2,1)S(1)} %get-tuple-element.20), channel_id=1, source_target_pairs={{0,8},{8,16},{16,24},{1,9},{9,17},{17,25},{2,10},{10,18},{18,26},{... | collective-permute-start | bytes 196616 | tf_op jit(solution)/shard_map/ppermute | solution.py:13
  264.3 96.6 %reduce-scatter.16.cloned.1.call-start = ((), (), s32[]{:S(2)}) async-start(), calls=%async_computation.11 | async-start | bytes 1179648 | tf_op jit(solution)/shard_map/reduce_scatter | solution.py:65
  296.7 5.5 %collective-permute-start.3 = (bf16[16,2048]{1,0:T(8,128)(2,1)S(1)}, bf16[16,2048]{1,0:T(8,128)(2,1)S(1)}, u32[]{:S(2)}, u32[]{:S(2)}) collective-permute-start(bf16[16,2048]{1,0:T(8,128)(2,1)S(1)} %get-tuple-element.16), channel_id=1, source_target_pairs={{0,8},{8,16},{16,24},{1,9},{9,17},{17,25},{2,10},{10,18},{18,26},{... | collective-permute-start | bytes 196616 | tf_op jit(solution)/shard_map/ppermute | solution.py:13
  329.2 96.4 %reduce-scatter.18.cloned.1.call-start = ((), (), s32[]{:S(2)}) async-start(), calls=%async_computation.12 | async-start | bytes 1179648 | tf_op jit(solution)/shard_map/reduce_scatter | solution.py:65
  361.8 5.2 %collective-permute-start.4 = (bf16[16,2048]{1,0:T(8,128)(2,1)S(1)}, bf16[16,2048]{1,0:T(8,128)(2,1)S(1)}, u32[]{:S(2)}, u32[]{:S(2)}) collective-permute-start(bf16[16,2048]{1,0:T(8,128)(2,1)S(1)} %get-tuple-element.12), channel_id=1, source_target_pairs={{0,8},{8,16},{16,24},{1,9},{9,17},{17,25},{2,10},{10,18},{18,26},{... | collective-permute-start | bytes 196616 | tf_op jit(solution)/shard_map/ppermute | solution.py:13
  394.1 96.3 %reduce-scatter.20.cloned.1.call-start = ((), (), s32[]{:S(2)}) async-start(), calls=%async_computation.13 | async-start | bytes 1179648 | tf_op jit(solution)/shard_map/reduce_scatter | solution.py:65
  426.5 5.6 %collective-permute-start.5 = (bf16[16,2048]{1,0:T(8,128)(2,1)S(1)}, bf16[16,2048]{1,0:T(8,128)(2,1)S(1)}, u32[]{:S(2)}, u32[]{:S(2)}) collective-permute-start(bf16[16,2048]{1,0:T(8,128)(2,1)S(1)} %get-tuple-element.8), channel_id=1, source_target_pairs={{0,8},{8,16},{16,24},{1,9},{9,17},{17,25},{2,10},{10,18},{18,26},{... | collective-permute-start | bytes 196616 | tf_op jit(solution)/shard_map/ppermute | solution.py:13
Sparse Core Ops, SparseCore 0:
  67.4 33.7 reduce-scatter.7
  134.5 31.4 reduce-scatter.9
  199.2 31.6 reduce-scatter.11
  264.4 31.3 reduce-scatter.13
  329.3 31.5 reduce-scatter.15
  394.2 31.3 reduce-scatter.17
  459.0 31.2 reduce-scatter.19
where the time goes:
time: 500 us; the launch traced here: 499 us
  waiting for transfers between devices  234 us (47%)
  blocking collectives  135 us (27%)
  matrix products  80.9 us (16%)
  starting transfers between devices  21.1 us (4%)
  between operations  13.8 us (3%)
  other arithmetic  11.1 us (2%)
    reduce_scatter x7, waiting for transfers between devices, on_device(): mixed = lax.psum_scatter(partial, 'expert', scatter_dimension=0, tiled=True)  223 us
    all_gather x7, blocking collectives, on_device(): rows = lax.all_gather(normed, 'expert', axis=0, tiled=True)  105 us
    dot_general x7, matrix products, on_device(): jnp.einsum('etf,efd->etd', inner, w_down, preferred_element_type=jnp.floa...  54.5 us
    dot_general x7, matrix products, on_device(): jnp.einsum('td,edf->etf', rows, w_gate, preferred_element_type=jnp.float32)  26.4 us
    ppermute x6, starting transfers between devices, shifted(): return lax.ppermute(array, axis, pairs)  20.8 us
    all_gather x1, blocking collectives, on_device(): all_gates = lax.all_gather(gates[0], 'expert', axis=1, tiled=True)  15.9 us
    all_gather x1, blocking collectives, on_device(): all_routes = lax.all_gather(routes[0], 'expert', axis=1, tiled=True)  14.2 us
    ppermute x6, waiting for transfers between devices, shifted(): return lax.ppermute(array, axis, pairs)  11.3 us
  transfers between devices with their start and end apart: 13, of which 13 were waited for; matrix products, arithmetic and copies ran while one was open for 0% of the time, Pallas kernels for 0%

commit v1 on v0

--- a/solution.py
+++ b/solution.py
@@ -54,7 +54,16 @@
         incoming = jnp.where(section_index == 0, first_rows, arrived)
         weight = lax.dynamic_index_in_dim(mixing, clipped, 0, keepdims=False)
         values, normed = rms_normed(incoming, gain)
-        rows = lax.all_gather(normed, "expert", axis=0, tiled=True)
+        ring = [normed]
+        for hop in range(7):
+            ring.append(
+                lax.ppermute(ring[-1], "expert", [(dev, (dev + 1) % 8) for dev in range(8)])
+            )
+        rows = jnp.roll(
+            jnp.concatenate(ring[::-1], axis=0),
+            (lax.axis_index("expert") + 1) * ring[0].shape[0],
+            axis=0,
+        )
         gate_part = jnp.einsum("td,edf->etf", rows, w_gate, preferred_element_type=jnp.float32)
         up_part = jnp.einsum("td,edf->etf", rows, w_up, preferred_element_type=jnp.float32)
         inner = (jax.nn.silu(gate_part) * up_part).astype(jnp.bfloat16)

time: 500 us -> 653 us (1.31)
  waiting for transfers between devices: 234 us -> 488 us
  blocking collectives: 135 us -> 28.5 us
    ppermute x0 -> x49, waiting for transfers between devices: none -> 258 us  [on_device(): lax.ppermute(ring[-1], 'expert', [(dev, (dev + 1) % 8) for dev in range(8)])]
    all_gather x7 -> x0, blocking collectives: 105 us -> none  [on_device(): rows = lax.all_gather(normed, 'expert', axis=0, tiled=True)]
  transfers between devices with their start and end apart: 13 -> 62, of which waited for: 13 -> 60; matrix products, arithmetic and copies ran while one was open for 0% -> 0% of each run, Pallas kernels for 0% -> 0%
where the time goes in v1:
time: 653 us; the launch traced here: 652 us
  waiting for transfers between devices  488 us (75%)
  matrix products  82.6 us (13%)
  blocking collectives  28.5 us (4%)
  starting transfers between devices  23.8 us (4%)
  between operations  14.2 us (2%)
  other arithmetic  12.5 us (2%)
    ppermute x49, waiting for transfers between devices, on_device(): lax.ppermute(ring[-1], 'expert', [(dev, (dev + 1) % 8) for dev in range(8)])  258 us
    reduce_scatter x7, waiting for transfers between devices, on_device(): mixed = lax.psum_scatter(partial, 'expert', scatter_dimension=0, tiled=True)  219 us
    dot_general x7, matrix products, on_device(): jnp.einsum('etf,efd->etd', inner, w_down, preferred_element_type=jnp.floa...  55.3 us
    dot_general x7, matrix products, on_device(): jnp.einsum('td,edf->etf', rows, w_gate, preferred_element_type=jnp.float32)  27.2 us
    ppermute x6, starting transfers between devices, shifted(): return lax.ppermute(array, axis, pairs)  21.5 us
    all_gather x1, blocking collectives, on_device(): all_gates = lax.all_gather(gates[0], 'expert', axis=1, tiled=True)  14.4 us
    all_gather x1, blocking collectives, on_device(): all_routes = lax.all_gather(routes[0], 'expert', axis=1, tiled=True)  14.2 us
  transfers between devices with their start and end apart: 62, of which 60 were waited for; matrix products, arithmetic and copies ran while one was open for 0% of the time, Pallas kernels for 0%

profile of v1, /device:TPU:0, one launch (start us, length us, event | category | flops | bytes accessed | tf_op | source)
XLA Modules:
  0.0 652.4 jit_solution(10869019666607176222)
XLA Ops:
  9.0 6.0 collective-permute-done
  15.0 5.5 collective-permute-done.1
  21.2 14.4 %all-gather.1 = f32[1,4,128,8]{3,1,0,2:T(4,128)S(1)} all-gather(f32[1,4,16,8]{3,1,0,2:T(4,128)S(1)} %copy.16), channel_id=3, replica_groups=mesh['section'=4,'expert'=8] {'expert'}, dimensions={2}, use_global_device_ids=true | all-gather | bytes 18432 | tf_op jit(solution)/shard_map/all_gather | solution.py:39
  37.4 14.2 %all-gather = s32[1,4,128,8]{3,1,0,2:T(4,128)S(1)} all-gather(s32[1,4,16,8]{3,1,0,2:T(4,128)S(1)} %copy.14), channel_id=2, replica_groups=mesh['section'=4,'expert'=8] {'expert'}, dimensions={2}, use_global_device_ids=true | all-gather | bytes 18432 | tf_op jit(solution)/shard_map/all_gather | solution.py:38
  73.1 7.9 %fusion.123 = f32[128,2048]{1,0:T(8,128)} fusion(bf16[1,2,768,2048]{3,2,1,0:T(8,128)(2,1)} %param.13, f32[2,128]{1,0:T(2,128)S(1)} %get-tuple-element.36, bf16[1,2,2048,768]{3,2,1,0:T(8,128)(2,1)} %param.12, f32[2,128,768]{2,1,0:T(8,128)S(1)} %fusion.126, s32[]{:T(128)S(6)} %select_n.252, bf16[128,2048]{1,0:T(8,128)(2,1)S(1)} %constant_dynamic-update-slice_fusion), kind=kOutput, calls=%fused_computation.69 | convolution fusion | flops 1614675968 | bytes 14943236 | tf_op jit(solution)/shard_map/etf,efd->etd/dot_general | solution.py:70
  81.1 31.0 %reduce-scatter.8.cloned.1.call-done = f32[16,2048]{1,0:T(8,128)} async-done(((f32[128,2048]{1,0:T(8,128)}), f32[16,2048]{1,0:T(8,128)}) %reduce-scatter.8.cloned.1.call-update) | async-done | bytes 131088 | tf_op jit(solution)/shard_map/reduce_scatter | solution.py:74
  124.5 5.5 collective-permute-done.9
  130.0 5.5 collective-permute-done.10
  135.5 5.5 collective-permute-done.11
  141.0 5.5 collective-permute-done.12
  146.5 5.5 collective-permute-done.13
  152.0 5.5 collective-permute-done.14
  161.5 7.9 %fusion.120 = f32[128,2048]{1,0:T(8,128)} fusion(bf16[1,2,768,2048]{3,2,1,0:T(8,128)(2,1)} %param.13, f32[2,128]{1,0:T(2,128)S(1)} %get-tuple-element.35, bf16[1,2,2048,768]{3,2,1,0:T(8,128)(2,1)} %param.12, f32[2,128,768]{2,1,0:T(8,128)S(1)} %fusion.129, s32[]{:T(128)S(6)} %select_n.252, bf16[128,2048]{1,0:T(8,128)(2,1)S(1)} %constant_dynamic-update-slice_fusion.8), kind=kOutput, calls=%fused_computation.68 | convolution fusion | flops 1614675968 | bytes 14943236 | tf_op jit(solution)/shard_map/etf,efd->etd/dot_general | solution.py:70
  169.4 31.3 %reduce-scatter.10.cloned.1.call-done = f32[16,2048]{1,0:T(8,128)} async-done(((f32[128,2048]{1,0:T(8,128)}), f32[16,2048]{1,0:T(8,128)}) %reduce-scatter.10.cloned.1.call-update) | async-done | bytes 131088 | tf_op jit(solution)/shard_map/reduce_scatter | solution.py:74
  213.0 5.5 collective-permute-done.17
  218.5 5.5 collective-permute-done.18
  224.0 5.5 collective-permute-done.19
  229.5 5.5 collective-permute-done.20
  235.0 5.5 collective-permute-done.21
  240.5 5.5 collective-permute-done.22
  250.1 7.9 %fusion.117 = f32[128,2048]{1,0:T(8,128)} fusion(bf16[1,2,768,2048]{3,2,1,0:T(8,128)(2,1)} %param.13, f32[2,128]{1,0:T(2,128)S(1)} %get-tuple-element.34, bf16[1,2,2048,768]{3,2,1,0:T(8,128)(2,1)} %param.12, f32[2,128,768]{2,1,0:T(8,128)S(1)} %fusion.132, s32[]{:T(128)S(6)} %select_n.252, bf16[128,2048]{1,0:T(8,128)(2,1)S(1)} %constant_dynamic-update-slice_fusion.16), kind=kOutput, calls=%fused_computation.67 | convolution fusion | flops 1614675968 | bytes 14943236 | tf_op jit(solution)/shard_map/etf,efd->etd/dot_general | solution.py:70
  258.1 31.5 %reduce-scatter.12.cloned.1.call-done = f32[16,2048]{1,0:T(8,128)} async-done(((f32[128,2048]{1,0:T(8,128)}), f32[16,2048]{1,0:T(8,128)}) %reduce-scatter.12.cloned.1.call-update) | async-done | bytes 131088 | tf_op jit(solution)/shard_map/reduce_scatter | solution.py:74
  301.7 5.5 collective-permute-done.25
  307.2 5.5 collective-permute-done.26
  312.7 5.5 collective-permute-done.27
  318.2 5.5 collective-permute-done.28
  323.7 5.5 collective-permute-done.29
  329.2 5.5 collective-permute-done.30
  338.7 7.9 %fusion.114 = f32[128,2048]{1,0:T(8,128)} fusion(bf16[1,2,768,2048]{3,2,1,0:T(8,128)(2,1)} %param.13, f32[2,128]{1,0:T(2,128)S(1)} %get-tuple-element.33, bf16[1,2,2048,768]{3,2,1,0:T(8,128)(2,1)} %param.12, f32[2,128,768]{2,1,0:T(8,128)S(1)} %fusion.135, s32[]{:T(128)S(6)} %select_n.252, bf16[128,2048]{1,0:T(8,128)(2,1)S(1)} %constant_dynamic-update-slice_fusion.24), kind=kOutput, calls=%fused_computation.66 | convolution fusion | flops 1614675968 | bytes 14943236 | tf_op jit(solution)/shard_map/etf,efd->etd/dot_general | solution.py:70
  346.8 31.2 %reduce-scatter.14.cloned.1.call-done = f32[16,2048]{1,0:T(8,128)} async-done(((f32[128,2048]{1,0:T(8,128)}), f32[16,2048]{1,0:T(8,128)}) %reduce-scatter.14.cloned.1.call-update) | async-done | bytes 131088 | tf_op jit(solution)/shard_map/reduce_scatter | solution.py:74
  390.2 5.5 collective-permute-done.33
  395.7 5.5 collective-permute-done.34
  401.2 5.5 collective-permute-done.35
  406.6 5.5 collective-permute-done.36
  412.1 5.5 collective-permute-done.37
  417.6 5.5 collective-permute-done.38
  427.2 7.9 %fusion.111 = f32[128,2048]{1,0:T(8,128)} fusion(bf16[1,2,768,2048]{3,2,1,0:T(8,128)(2,1)} %param.13, f32[2,128]{1,0:T(2,128)S(1)} %get-tuple-element.32, bf16[1,2,2048,768]{3,2,1,0:T(8,128)(2,1)} %param.12, f32[2,128,768]{2,1,0:T(8,128)S(1)} %fusion.138, s32[]{:T(128)S(6)} %select_n.252, bf16[128,2048]{1,0:T(8,128)(2,1)S(1)} %constant_dynamic-update-slice_fusion.32), kind=kOutput, calls=%fused_computation.65 | convolution fusion | flops 1614675968 | bytes 14943236 | tf_op jit(solution)/shard_map/etf,efd->etd/dot_general | solution.py:70
  435.2 31.5 %reduce-scatter.16.cloned.1.call-done = f32[16,2048]{1,0:T(8,128)} async-done(((f32[128,2048]{1,0:T(8,128)}), f32[16,2048]{1,0:T(8,128)}) %reduce-scatter.16.cloned.1.call-update) | async-done | bytes 131088 | tf_op jit(solution)/shard_map/reduce_scatter | solution.py:74
  479.0 5.5 collective-permute-done.41
  484.5 5.5 collective-permute-done.42
  501.0 5.5 collective-permute-done.45
  516.0 7.9 %fusion.108 = f32[128,2048]{1,0:T(8,128)} fusion(bf16[1,2,768,2048]{3,2,1,0:T(8,128)(2,1)} %param.13, f32[2,128]{1,0:T(2,128)S(1)} %get-tuple-element.31, bf16[1,2,2048,768]{3,2,1,0:T(8,128)(2,1)} %param.12, f32[2,128,768]{2,1,0:T(8,128)S(1)} %fusion.141, s32[]{:T(128)S(6)} %select_n.252, bf16[128,2048]{1,0:T(8,128)(2,1)S(1)} %constant_dynamic-update-slice_fusion.40), kind=kOutput, calls=%fused_computation.64 | convolution fusion | flops 1614675968 | bytes 14943236 | tf_op jit(solution)/shard_map/etf,efd->etd/dot_general | solution.py:70
  524.0 31.3 %reduce-scatter.18.cloned.1.call-done = f32[16,2048]{1,0:T(8,128)} async-done(((f32[128,2048]{1,0:T(8,128)}), f32[16,2048]{1,0:T(8,128)}) %reduce-scatter.18.cloned.1.call-update) | async-done | bytes 131088 | tf_op jit(solution)/shard_map/reduce_scatter | solution.py:74
  578.4 5.5 collective-permute-done.51
  583.9 5.5 collective-permute-done.52
  594.8 5.5 collective-permute-done.54
  604.4 7.9 %fusion.105 = f32[128,2048]{1,0:T(8,128)} fusion(bf16[1,2,768,2048]{3,2,1,0:T(8,128)(2,1)} %param.13, f32[2,128]{1,0:T(2,128)S(1)} %get-tuple-element.30, bf16[1,2,2048,768]{3,2,1,0:T(8,128)(2,1)} %param.12, f32[2,128,768]{2,1,0:T(8,128)S(1)} %fusion.144, s32[]{:T(128)S(6)} %select_n.252, bf16[128,2048]{1,0:T(8,128)(2,1)S(1)} %constant_dynamic-update-slice_fusion.48), kind=kOutput, calls=%fused_computation.63 | convolution fusion | flops 1614675968 | bytes 14943236 | tf_op jit(solution)/shard_map/etf,efd->etd/dot_general | solution.py:70
  613.0 31.0 %reduce-scatter.20.cloned.1.call-done = f32[16,2048]{1,0:T(8,128)} async-done(((f32[128,2048]{1,0:T(8,128)}), f32[16,2048]{1,0:T(8,128)}) %reduce-scatter.20.cloned.1.call-update) | async-done | bytes 131088 | tf_op jit(solution)/shard_map/reduce_scatter | solution.py:74
  (198 shorter events, 159.5 us)
Async XLA Ops:
  6.5 105.6 %reduce-scatter.8.cloned.1.call-start = ((), (), s32[]{:S(2)}) async-start(), calls=%async_computation.7 | async-start | bytes 1179648 | tf_op jit(solution)/shard_map/reduce_scatter | solution.py:74
  8.5 6.5 collective-permute-start
  15.0 5.5 collective-permute-start.1
  20.4 15.4 %collective-permute-start.2 = (bf16[16,2048]{1,0:T(8,128)(2,1)S(1)}, bf16[16,2048]{1,0:T(8,128)(2,1)S(1)}, u32[]{:S(2)}, u32[]{:S(2)}) collective-permute-start(bf16[16,2048]{1,0:T(8,128)(2,1)S(1)} %collective-permute-done.1), channel_id=1, source_target_pairs={{0,1},{1,2},{2,3},{3,4},{4,5},{5,6},{6,7},{7,0},{8,9},{9,10},{10,1... | collective-permute-start | bytes 196616 | tf_op jit(solution)/shard_map/ppermute | solution.py:60
  35.8 15.8 %collective-permute-start.3 = (bf16[16,2048]{1,0:T(8,128)(2,1)S(1)}, bf16[16,2048]{1,0:T(8,128)(2,1)S(1)}, u32[]{:S(2)}, u32[]{:S(2)}) collective-permute-start(bf16[16,2048]{1,0:T(8,128)(2,1)S(1)} %collective-permute-done.2), channel_id=1, source_target_pairs={{0,1},{1,2},{2,3},{3,4},{4,5},{5,6},{6,7},{7,0},{8,9},{9,10},{10,1... | collective-permute-start | bytes 196616 | tf_op jit(solution)/shard_map/ppermute | solution.py:60
  51.7 5.5 collective-permute-start.4
  57.2 5.5 collective-permute-start.5
  62.7 5.5 collective-permute-start.6
  81.1 119.7 %reduce-scatter.10.cloned.1.call-start = ((), (), s32[]{:S(2)}) async-start(), calls=%async_computation.8 | async-start | bytes 1179648 | tf_op jit(solution)/shard_map/reduce_scatter | solution.py:74
  113.1 5.6 collective-permute-start.7
  119.0 5.5 collective-permute-start.8
  124.5 5.5 collective-permute-start.9
  130.0 5.5 collective-permute-start.10
  135.5 5.5 collective-permute-start.11
  141.0 5.5 collective-permute-start.12
  146.5 5.5 collective-permute-start.13
  152.0 5.5 collective-permute-start.14
  169.4 120.2 %reduce-scatter.12.cloned.1.call-start = ((), (), s32[]{:S(2)}) async-start(), calls=%async_computation.9 | async-start | bytes 1179648 | tf_op jit(solution)/shard_map/reduce_scatter | solution.py:74
  201.7 5.6 collective-permute-start.15
  207.5 5.5 collective-permute-start.16
  213.0 5.5 collective-permute-start.17
  218.5 5.5 collective-permute-start.18
  224.0 5.5 collective-permute-start.19
  229.5 5.5 collective-permute-start.20
  235.0 5.5 collective-permute-start.21
  240.5 5.5 collective-permute-start.22
  258.0 119.9 %reduce-scatter.14.cloned.1.call-start = ((), (), s32[]{:S(2)}) async-start(), calls=%async_computation.10 | async-start | bytes 1179648 | tf_op jit(solution)/shard_map/reduce_scatter | solution.py:74
  296.2 5.5 collective-permute-start.24
  301.7 5.5 collective-permute-start.25
  307.2 5.5 collective-permute-start.26
  312.7 5.5 collective-permute-start.27
  318.2 5.5 collective-permute-start.28
  323.7 5.5 collective-permute-start.29
  329.2 5.5 collective-permute-start.30
  346.7 119.9 %reduce-scatter.16.cloned.1.call-start = ((), (), s32[]{:S(2)}) async-start(), calls=%async_computation.11 | async-start | bytes 1179648 | tf_op jit(solution)/shard_map/reduce_scatter | solution.py:74
  378.9 5.5 collective-permute-start.31
  384.6 5.5 collective-permute-start.32
  390.2 5.5 collective-permute-start.33
  395.7 5.5 collective-permute-start.34
  412.1 5.5 collective-permute-start.37
  435.1 120.2 %reduce-scatter.18.cloned.1.call-start = ((), (), s32[]{:S(2)}) async-start(), calls=%async_computation.12 | async-start | bytes 1179648 | tf_op jit(solution)/shard_map/reduce_scatter | solution.py:74
  473.3 5.8 collective-permute-start.40
  484.5 5.5 collective-permute-start.42
  501.0 5.5 collective-permute-start.45
  523.9 120.1 %reduce-scatter.20.cloned.1.call-start = ((), (), s32[]{:S(2)}) async-start(), calls=%async_computation.13 | async-start | bytes 1179648 | tf_op jit(solution)/shard_map/reduce_scatter | solution.py:74
  561.9 5.5 collective-permute-start.48
  578.4 5.5 collective-permute-start.51
  583.9 5.5 collective-permute-start.52
  (16 other events, 161.4 us)
Sparse Core Ops, SparseCore 0:
  81.2 30.9 reduce-scatter.7
  169.5 31.1 reduce-scatter.9
  258.1 31.4 reduce-scatter.11
  346.8 31.0 reduce-scatter.13
  435.3 31.3 reduce-scatter.15
  524.0 31.2 reduce-scatter.17
  612.4 31.5 reduce-scatter.19
